TPU v7x, 128 devices: a whole 4x4x4 slice. The times are simulated.
128 devices in a mesh: seq: 16 (over x_lo, z, core), batch: 8 (over y, x_hi).
Axes of the slice: x: 4 (x_hi: 2, x_lo: 2; x = x_hi * 2 + x_lo), y: 4, z: 4, core: 2. Of those that a mesh axis runs over, the one named last changes fastest.
Arguments:
- activations: bfloat16 [2, 8192, 1536], P(None, ('seq', 'batch')), may hold values from -6 to 6
- conv_gain: float32 [1536], replicated, may hold values from 0.25 to 1.75
- conv_weight: bfloat16 [5, 1536, 1536], P(None, 'batch'), may hold values from -0.0625 to 0.0625
- attention_gain: float32 [1536], replicated, may hold values from 0.25 to 1.75
- query_weight: bfloat16 [1536, 1536], P('batch'), may hold values from -3 to 3
- key_weight: bfloat16 [1536, 1536], P('batch'), may hold values from -3 to 3
- value_weight: bfloat16 [1536, 1536], P('batch'), may hold values from -0.15625 to 0.15625
- output_weight: bfloat16 [1536, 1536], P('batch'), may hold values from -0.15625 to 0.15625
Outputs:
- block_out: bfloat16 [2, 8192, 1536], P(None, ('seq', 'batch'))
All inputs are finite; a program needn't handle non-finite values.
Results may differ from a plain program's by a relative error of at most 0.015.
Values may be sent and summed in bfloat16 or wider, within the bound.
No kernel may reach another device: no remote copies, remote signals or barrier semaphores. Data moves between devices by JAX's collectives and lax.ppermute only.
A program may use at most 128 MiB of HBM per device.

v0:
```python
import math
import jax
import jax.numpy as jnp
from jax import lax
from jax.sharding import PartitionSpec as P

HD = 192


def with_halo(cells, sides, width):
    for axis, dim in sides:
        count = lax.axis_size(axis)
        ends = count - 1
        head = lax.slice_in_dim(cells, 0, width, axis=dim)
        tail = lax.slice_in_dim(cells, cells.shape[dim] - width, cells.shape[dim], axis=dim)
        cells = jnp.concatenate(
            [
                lax.ppermute(tail, axis, [(i, (i + 1) % count) for i in range(ends)]),
                cells,
                lax.ppermute(head, axis, [((i + 1) % count, i) for i in range(ends)]),
            ],
            axis=dim,
        )
    return cells


def gather_batch(block, axis):
    count = lax.axis_size("batch")
    copies = jnp.broadcast_to(block[None], (count,) + block.shape)
    arrived = jnp.moveaxis(lax.all_to_all(copies, "batch", 0, 0, tiled=False), 0, axis)
    return arrived.reshape(
        block.shape[:axis] + (count * block.shape[axis],) + block.shape[axis + 1 :]
    )


def normalize(rows_in, gain):
    values = rows_in.astype(jnp.float32)
    scale = lax.rsqrt(jnp.mean(values * values, axis=-1, keepdims=True) + 1e-06)
    return values * scale * gain


def one_sample(
    activations,
    conv_gain,
    conv_weight,
    attention_gain,
    query_weight,
    key_weight,
    value_weight,
    output_weight,
):
    sample_count, own_rows, full_width = activations.shape
    tap_count, local_out, _ = conv_weight.shape
    flank_rows = tap_count // 2
    gathered_in = gather_batch(activations, 1)
    seq_rows = gathered_in.shape[1]
    active = jax.nn.gelu(normalize(gathered_in, conv_gain)).astype(jnp.bfloat16)
    framed = with_halo(active, (("seq", 1),), flank_rows)
    conv_sum = jnp.zeros((sample_count, local_out, seq_rows), jnp.float32)
    for offset in range(tap_count):
        conv_sum = conv_sum + jnp.einsum(
            "std,ed->set",
            framed[:, offset : offset + seq_rows],
            conv_weight[offset],
            preferred_element_type=jnp.float32,
        )
    column_start = lax.axis_index("batch") * local_out
    own_columns = lax.dynamic_slice_in_dim(gathered_in, column_start, local_out, 2)
    residual = jnp.transpose(own_columns, (0, 2, 1)).astype(jnp.float32)
    hidden_part = (residual + conv_sum).astype(jnp.bfloat16)
    hidden_full = gather_batch(hidden_part, 1)
    hidden_float = hidden_full.astype(jnp.float32)
    norm_scale = lax.rsqrt(jnp.mean(hidden_float * hidden_float, axis=1, keepdims=True) + 1e-06)
    normed = (hidden_float * norm_scale * attention_gain[None, :, None]).astype(jnp.bfloat16)
    queries = (
        jnp.einsum("sdt,ed->set", normed, query_weight, preferred_element_type=jnp.float32)
        * HD ** (-0.5)
    ).astype(jnp.bfloat16)
    key_rows = jnp.einsum(
        "sdt,ed->set", normed, key_weight, preferred_element_type=jnp.float32
    ).astype(jnp.bfloat16)
    value_rows = jnp.einsum(
        "sdt,ed->set", normed, value_weight, preferred_element_type=jnp.float32
    ).astype(jnp.bfloat16)
    heads_here = query_weight.shape[0] // HD
    query_heads = queries.reshape(sample_count, heads_here, HD, seq_rows)
    start_max = jnp.full((sample_count, heads_here, seq_rows), -jnp.inf, jnp.float32)
    start_sum = jnp.zeros((sample_count, heads_here, seq_rows), jnp.float32)
    start_acc = jnp.zeros((sample_count, heads_here, HD, seq_rows), jnp.float32)
    key_tile = lax.all_gather(key_rows, "seq", axis=2, tiled=True)
    value_tile = lax.all_gather(value_rows, "seq", axis=2, tiled=True)
    key_count = key_tile.shape[2]
    block_rows = math.gcd(key_count, 512)

    def consume(block_index, running):
        running_max, weight_sum, summed = running
        begin = block_index * block_rows
        key_block = lax.dynamic_slice_in_dim(key_tile, begin, block_rows, 2).reshape(
            sample_count, heads_here, HD, block_rows
        )
        value_block = lax.dynamic_slice_in_dim(value_tile, begin, block_rows, 2).reshape(
            sample_count, heads_here, HD, block_rows
        )
        scores = jnp.einsum(
            "shdq,shdk->shqk", query_heads, key_block, preferred_element_type=jnp.float32
        )
        new_max = jnp.maximum(running_max, jnp.max(scores, axis=-1))
        weights = jnp.exp(scores - new_max[..., None])
        rescale = jnp.exp(running_max - new_max)
        weight_sum = weight_sum * rescale + jnp.sum(weights, axis=-1)
        summed = summed * rescale[:, :, None, :] + jnp.einsum(
            "shqk,shdk->shdq",
            weights.astype(jnp.bfloat16),
            value_block,
            preferred_element_type=jnp.float32,
        )
        return (new_max, weight_sum, summed)

    final_max, weight_sum, summed = lax.fori_loop(
        0, key_count // block_rows, consume, (start_max, start_sum, start_acc)
    )
    attended = (
        (summed / weight_sum[:, :, None, :])
        .astype(jnp.bfloat16)
        .reshape(sample_count, heads_here * HD, seq_rows)
    )
    row_start = lax.axis_index("batch") * own_rows
    own_hidden = jnp.transpose(
        lax.dynamic_slice_in_dim(hidden_full, row_start, own_rows, 2), (0, 2, 1)
    ).astype(jnp.float32)
    batch_count = lax.axis_size("batch")
    partial_rows = jnp.einsum(
        "set,ef->tsf", attended, output_weight, preferred_element_type=jnp.float32
    ).astype(jnp.bfloat16)
    partial_rows = partial_rows.reshape(batch_count, own_rows, sample_count, full_width)
    share_rows = jnp.sum(
        lax.all_to_all(partial_rows, "batch", 0, 0, tiled=False).astype(jnp.float32), axis=0
    )
    branch_rows = jnp.transpose(share_rows, (1, 0, 2))
    result = own_hidden + branch_rows
    return result.astype(jnp.bfloat16)


def shards(activations, *weights):
    pieces = [
        one_sample(activations[sample : sample + 1], *weights)
        for sample in range(activations.shape[0])
    ]
    return jnp.concatenate(pieces, axis=0)


def solution(mesh):
    placed = (
        P(None, ("seq", "batch"), None),
        P(),
        P(None, "batch", None),
        P(),
        P("batch", None),
        P("batch", None),
        P("batch", None),
        P("batch", None),
    )
    return jax.shard_map(
        shards,
        mesh=mesh,
        in_specs=placed,
        out_specs=P(None, ("seq", "batch"), None),
        check_vma=False,
    )
```

profile of v0, /device:TPU:0, one launch (start us, length us, event | category | flops | bytes accessed | tf_op | source)
XLA Modules:
  0.0 390.3 jit_solution(14848912916177011553)
XLA Ops:
  7.8 29.6 %all_to_all.30 = bf16[8,1,64,1536]{3,2,1,0:T(8,128)(2,1)S(1)} all-to-all(bf16[8,1,64,1536]{3,2,1,0:T(8,128)(2,1)S(1)} %broadcast_in_dim.27), channel_id=1, replica_groups=mesh['seq'=16,'batch'=8] {'batch'}, dimensions={0} | all-to-all | bytes 3145728 | tf_op jit(solution)/shard_map/all_to_all | solution.py:30
  38.7 4.4 %all-to-all-start.3 = ((bf16[8,1,64,1536]{3,2,1,0:T(8,128)(2,1)}), bf16[8,1,64,1536]{3,2,1,0:T(8,128)(2,1)}, u32[]{:S(2)}, u32[]{:S(2)}) async-start(bf16[8,1,64,1536]{3,2,1,0:T(8,128)(2,1)} %broadcast_in_dim.33), calls=%async_computation.3 | async-start | bytes 3145728 | tf_op jit(solution)/shard_map/all_to_all | solution.py:30
  43.6 21.5 %all-to-all-done.3 = bf16[8,1,64,1536]{3,2,1,0:T(8,128)(2,1)} async-done(((bf16[8,1,64,1536]{3,2,1,0:T(8,128)(2,1)}), bf16[8,1,64,1536]{3,2,1,0:T(8,128)(2,1)}, u32[]{:S(2)}, u32[]{:S(2)}) %all-to-all-start.3) | async-done | bytes 1572896 | tf_op jit(solution)/shard_map/all_to_all | solution.py:30
  65.1 1.8 fusion.41
  68.3 4.0 %fusion.57 = (bf16[1,512,1536]{2,1,0:T(8,128)(2,1)S(1)}, bf16[1,512,1536]{2,1,0:T(8,128)(2,1)S(1)}) fusion(bf16[1,512,1536]{2,1,0:T(8,128)(2,1)S(1)} %bitcast.299, f32[1536]{0:T(1024)S(1)} %copy-done.7, f32[512]{0:T(512)S(1)} %rsqrt.41, f32[512]{0:T(512)S(1)} %rsqrt.44, bf16[1,512,1536]{2,1,0:T(8,128)(2,1)} %bitcast.37), kind=kLoop, calls=%fused_computation.75 | loop fusion | flops 18874368 | bytes 6301696 | tf_op jit(solution)/shard_map/convert_element_type | solution.py:57
  74.9 1.6 collective-permute-start.1
  76.5 4.8 %fusion.36 = (bf16[8,1,64,1536]{3,2,0,1:T(8,128)(2,1)}, bf16[8,1,64,1536]{3,2,0,1:T(8,128)(2,1)S(1)}) fusion(bf16[8,1,64,1536]{3,2,1,0:T(8,128)(2,1)S(1)} %all_to_all.30, f32[1536]{0:T(1024)S(1)} %copy-done.7, f32[8,64]{1,0:T(8,128)S(1)} %add_rsqrt_fusion.1, f32[8,64]{1,0:T(8,128)S(1)} %add_rsqrt_fusion, bf16[8,1,64,1536]{3,2,1,0:T(8,128)(2,1)} %all-to-all-done.3), kind=kLoop, calls=%fused_computation.54 | loop fusion | flops 18874368 | bytes 6301696 | tf_op jit(solution)/shard_map/convert_element_type | solution.py:57
  85.9 4.3 %all-to-all-start.4 = ((bf16[8,1,192,512]{3,2,1,0:T(8,128)(2,1)}), bf16[8,1,192,512]{3,2,1,0:T(8,128)(2,1)}, u32[]{:S(2)}, u32[]{:S(2)}) async-start(bf16[8,1,192,512]{3,2,1,0:T(8,128)(2,1)} %broadcast_in_dim.61), calls=%async_computation.4 | async-start | bytes 3145728 | tf_op jit(solution)/shard_map/all_to_all | solution.py:30
  90.3 2.2 fusion.166
  92.8 6.1 %collective-permute-start = (bf16[1,2,1536]{2,1,0:T(2,128)(2,1)S(1)}, bf16[1,2,1536]{2,1,0:T(2,128)(2,1)S(1)}, u32[]{:S(2)}, u32[]{:S(2)}) collective-permute-start(bf16[1,2,1536]{2,1,0:T(2,128)(2,1)S(1)} %get-tuple-element.343), channel_id=1, source_target_pairs={{0,8},{8,16},{16,24},{24,32},{32,40},{40,48},{48,56},{56,64},{64,7... | collective-permute-start | bytes 18440 | tf_op jit(solution)/shard_map/ppermute | solution.py:18
  98.9 2.2 fusion.97
  103.2 8.3 %all-to-all-done.4 = bf16[8,1,192,512]{3,2,1,0:T(8,128)(2,1)} async-done(((bf16[8,1,192,512]{3,2,1,0:T(8,128)(2,1)}), bf16[8,1,192,512]{3,2,1,0:T(8,128)(2,1)}, u32[]{:S(2)}, u32[]{:S(2)}) %all-to-all-start.4) | async-done | bytes 1572896 | tf_op jit(solution)/shard_map/all_to_all | solution.py:30
  112.8 4.8 %all-to-all-start.1 = ((bf16[8,1,192,512]{3,2,1,0:T(8,128)(2,1)}), bf16[8,1,192,512]{3,2,1,0:T(8,128)(2,1)S(1)}, u32[]{:S(2)}, u32[]{:S(2)}) async-start(bf16[8,1,192,512]{3,2,1,0:T(8,128)(2,1)} %broadcast_in_dim.29), calls=%async_computation.1 | async-start | bytes 3145728 | tf_op jit(solution)/shard_map/all_to_all | solution.py:30
  117.8 1.8 multiply_reduce_fusion
  119.7 21.7 %all-to-all-done.1 = bf16[8,1,192,512]{3,2,1,0:T(8,128)(2,1)S(1)} async-done(((bf16[8,1,192,512]{3,2,1,0:T(8,128)(2,1)}), bf16[8,1,192,512]{3,2,1,0:T(8,128)(2,1)S(1)}, u32[]{:S(2)}, u32[]{:S(2)}) %all-to-all-start.1) | async-done | bytes 1572896 | tf_op jit(solution)/shard_map/all_to_all | solution.py:30
  142.5 1.8 bitcast_convert_fusion
  147.4 2.5 fusion.159
  151.3 1.5 fusion.149
  152.8 2.1 fusion.148
  154.9 2.2 fusion.157
  157.2 28.8 %all-gather.13.cloned.1.call-done = bf16[192,8192]{1,0:T(8,128)(2,1)} async-done(((bf16[192,512]{1,0:T(8,128)(2,1)}), bf16[192,8192]{1,0:T(8,128)(2,1)}) %all-gather.13.cloned.1.call-update) | async-done | bytes 3145744 | tf_op jit(solution)/shard_map/all_gather | solution.py:90
  186.0 37.6 %all-gather.15.cloned.1.call-done = bf16[192,8192]{1,0:T(8,128)(2,1)} async-done(((bf16[192,512]{1,0:T(8,128)(2,1)}), bf16[192,8192]{1,0:T(8,128)(2,1)}) %all-gather.15.cloned.1.call-update) | async-done | bytes 3145744 | tf_op jit(solution)/shard_map/all_gather | solution.py:91
  223.6 46.2 %while.37 = (s32[]{:T(128)}, f32[1,1,512]{2,1,0:T(1,128)S(1)}, f32[1,1,512]{2,1,0:T(1,128)S(1)}, f32[1,1,192,512]{3,2,1,0:T(8,128)S(1)}, bf16[1,192,8192]{2,1,0:...) while((s32[]{:T(128)}, f32[1,1,512]{2,1,0:T(1,128)S(1)}, ...), condition=%wide.region_12.0_spmd.clone, body=%wide.region_9.0_spmd.clone.sunk | while | flops 202934784 | bytes 4554935 | solution.py:119
  233.8 1.4 fusion.241
  269.8 1.8 convolution_convert_fusion
  271.6 6.4 %all-to-all-start.5 = ((bf16[8,64,1,1536]{3,1,2,0:T(8,128)(2,1)}), bf16[8,64,1,1536]{3,1,2,0:T(8,128)(2,1)S(1)}, u32[]{:S(2)}, u32[]{:S(2)}) async-start(bf16[8,64,1,1536]{3,1,2,0:T(8,128)(2,1)} %bitcast.302), calls=%async_computation.5 | async-start | bytes 3145728 | tf_op jit(solution)/shard_map/all_to_all | solution.py:137
  278.0 25.9 %all-gather.11.cloned.1.call-done = bf16[192,8192]{1,0:T(8,128)(2,1)} async-done(((bf16[192,512]{1,0:T(8,128)(2,1)}), bf16[192,8192]{1,0:T(8,128)(2,1)}) %all-gather.11.cloned.1.call-update) | async-done | bytes 3145744 | tf_op jit(solution)/shard_map/all_gather | solution.py:91
  303.9 46.1 %while.36 = (s32[]{:T(128)}, f32[1,1,512]{2,1,0:T(1,128)S(1)}, f32[1,1,512]{2,1,0:T(1,128)S(1)}, f32[1,1,192,512]{3,2,1,0:T(8,128)S(1)}, bf16[1,192,8192]{2,1,0:...) while((s32[]{:T(128)}, f32[1,1,512]{2,1,0:T(1,128)S(1)}, ...), condition=%wide.region_5.0_spmd.clone, body=%wide.region_2.0_spmd.clone.sunk | while | flops 202934784 | bytes 4554935 | solution.py:119
  350.0 1.9 convolution_convert_fusion.1
  351.9 6.0 %all-to-all-start.2 = ((bf16[8,64,1,1536]{3,1,2,0:T(8,128)(2,1)}), bf16[8,64,1,1536]{3,1,2,0:T(8,128)(2,1)}, u32[]{:S(2)}, u32[]{:S(2)}) async-start(bf16[8,64,1,1536]{3,1,2,0:T(8,128)(2,1)} %bitcast.303), calls=%async_computation.2 | async-start | bytes 3145728 | tf_op jit(solution)/shard_map/all_to_all | solution.py:137
  360.8 20.4 %all-to-all-done.2 = bf16[8,64,1,1536]{3,1,2,0:T(8,128)(2,1)} async-done(((bf16[8,64,1,1536]{3,1,2,0:T(8,128)(2,1)}), bf16[8,64,1,1536]{3,1,2,0:T(8,128)(2,1)}, u32[]{:S(2)}, u32[]{:S(2)}) %all-to-all-start.2) | async-done | bytes 1572896 | tf_op jit(solution)/shard_map/all_to_all | solution.py:137
  381.3 1.7 convert_reduce_fusion.1
  (274 shorter events, 114.1 us)
Async XLA Ops:
  6.5 263.3 %copy-start = (bf16[192,1536]{1,0:T(8,128)(2,1)S(1)}, bf16[192,1536]{1,0:T(8,128)(2,1)}, u32[]{:S(2)}) copy-start(bf16[192,1536]{1,0:T(8,128)(2,1)} %param.19) | copy-start | bytes 1769476
  38.7 29.5 %copy-start.7 = (f32[1536]{0:T(1024)S(1)}, f32[1536]{0:T(1024)}, u32[]{:S(2)}) copy-start(f32[1536]{0:T(1024)} %param.13) | copy-start | bytes 18436
  38.7 26.4 %all-to-all-start.3 = ((bf16[8,1,64,1536]{3,2,1,0:T(8,128)(2,1)}), bf16[8,1,64,1536]{3,2,1,0:T(8,128)(2,1)}, u32[]{:S(2)}, u32[]{:S(2)}) async-start(bf16[8,1,64,1536]{3,2,1,0:T(8,128)(2,1)} %broadcast_in_dim.33), calls=%async_computation.3 | async-start | bytes 3145728 | tf_op jit(solution)/shard_map/all_to_all | solution.py:30
  72.2 9.0 %copy-start.5 = (bf16[1,512,1536]{2,1,0:T(8,128)(2,1)}, bf16[1,512,1536]{2,1,0:T(8,128)(2,1)S(1)}, u32[]{:S(2)}) copy-start(bf16[1,512,1536]{2,1,0:T(8,128)(2,1)S(1)} %get-tuple-element.353) | copy-start | bytes 4718596
  72.3 11.0 %collective-permute-start.2 = (bf16[1,2,1536]{2,1,0:T(2,128)(2,1)S(1)}, bf16[1,2,1536]{2,1,0:T(2,128)(2,1)S(1)}, u32[]{:S(2)}, u32[]{:S(2)}) collective-permute-start(bf16[1,2,1536]{2,1,0:T(2,128)(2,1)S(1)} %get-tuple-element.345), channel_id=1, source_target_pairs={{0,8},{8,16},{16,24},{24,32},{32,40},{40,48},{48,56},{56,64},{64,7... | collective-permute-start | bytes 18440 | tf_op jit(solution)/shard_map/ppermute | solution.py:18
  73.6 8.3 %collective-permute-start.3 = (bf16[1,2,1536]{2,1,0:T(2,128)(2,1)S(1)}, bf16[1,2,1536]{2,1,0:T(2,128)(2,1)S(1)}, u32[]{:S(2)}, u32[]{:S(2)}) collective-permute-start(bf16[1,2,1536]{2,1,0:T(2,128)(2,1)S(1)} %get-tuple-element.346), channel_id=1, source_target_pairs={{8,0},{16,8},{24,16},{32,24},{40,32},{48,40},{56,48},{64,56},{72,6... | collective-permute-start | bytes 18440 | tf_op jit(solution)/shard_map/ppermute | solution.py:20
  74.9 6.4 %copy-start.9 = (bf16[5,192,1536]{2,1,0:T(8,128)(2,1)S(1)}, bf16[5,192,1536]{2,1,0:T(8,128)(2,1)}, u32[]{:S(2)}) copy-start(bf16[5,192,1536]{2,1,0:T(8,128)(2,1)} %param.14) | copy-start | bytes 8847364
  74.9 24.0 %collective-permute-start.1 = (bf16[1,2,1536]{2,1,0:T(2,128)(2,1)S(1)}, bf16[1,2,1536]{2,1,0:T(2,128)(2,1)S(1)}, u32[]{:S(2)}, u32[]{:S(2)}) collective-permute-start(bf16[1,2,1536]{2,1,0:T(2,128)(2,1)S(1)} %get-tuple-element.344), channel_id=1, source_target_pairs={{8,0},{16,8},{24,16},{32,24},{40,32},{48,40},{56,48},{64,56},{72,6... | collective-permute-start | bytes 18440 | tf_op jit(solution)/shard_map/ppermute | solution.py:20
  85.9 25.6 %all-to-all-start.4 = ((bf16[8,1,192,512]{3,2,1,0:T(8,128)(2,1)}), bf16[8,1,192,512]{3,2,1,0:T(8,128)(2,1)}, u32[]{:S(2)}, u32[]{:S(2)}) async-start(bf16[8,1,192,512]{3,2,1,0:T(8,128)(2,1)} %broadcast_in_dim.61), calls=%async_computation.4 | async-start | bytes 3145728 | tf_op jit(solution)/shard_map/all_to_all | solution.py:30
  92.6 8.5 %copy-start.6 = (bf16[1,512,1536]{2,1,0:T(8,128)(2,1)S(1)}, bf16[1,512,1536]{2,1,0:T(8,128)(2,1)}, u32[]{:S(2)}) copy-start(bf16[1,512,1536]{2,1,0:T(8,128)(2,1)} %copy-done.5) | copy-start | bytes 4718596
  92.8 8.4 %copy-start.10 = (bf16[5,192,1536]{2,1,0:T(8,128)(2,1)S(1)}, bf16[5,192,1536]{2,1,0:T(8,128)(2,1)}, u32[]{:S(2)}) copy-start(bf16[5,192,1536]{2,1,0:T(8,128)(2,1)} %param.14) | copy-start | bytes 8847364
  92.8 8.3 %collective-permute-start = (bf16[1,2,1536]{2,1,0:T(2,128)(2,1)S(1)}, bf16[1,2,1536]{2,1,0:T(2,128)(2,1)S(1)}, u32[]{:S(2)}, u32[]{:S(2)}) collective-permute-start(bf16[1,2,1536]{2,1,0:T(2,128)(2,1)S(1)} %get-tuple-element.343), channel_id=1, source_target_pairs={{0,8},{8,16},{16,24},{24,32},{32,40},{40,48},{48,56},{56,64},{64,7... | collective-permute-start | bytes 18440 | tf_op jit(solution)/shard_map/ppermute | solution.py:18
  112.8 28.6 %all-to-all-start.1 = ((bf16[8,1,192,512]{3,2,1,0:T(8,128)(2,1)}), bf16[8,1,192,512]{3,2,1,0:T(8,128)(2,1)S(1)}, u32[]{:S(2)}, u32[]{:S(2)}) async-start(bf16[8,1,192,512]{3,2,1,0:T(8,128)(2,1)} %broadcast_in_dim.29), calls=%async_computation.1 | async-start | bytes 3145728 | tf_op jit(solution)/shard_map/all_to_all | solution.py:30
  117.6 68.4 %all-gather.13.cloned.1.call-start = ((), (), s32[]{:S(2)}) async-start(), calls=%async_computation.8 | async-start | bytes 3342336 | tf_op jit(solution)/shard_map/all_gather | solution.py:90
  141.4 1.2 copy-start.2
  142.5 1.9 copy-start.8
  144.4 1.8 copy-start.3
  144.4 3.0 copy-start.4
  145.0 1.2 copy-start.1
  147.3 76.3 %all-gather.15.cloned.1.call-start = ((), (), s32[]{:S(2)}) async-start(), calls=%async_computation.9 | async-start | bytes 3342336 | tf_op jit(solution)/shard_map/all_gather | solution.py:91
  150.0 128.0 %all-gather.9.cloned.1.call-start = ((), (), s32[]{:S(2)}) async-start(), calls=%async_computation.6 | async-start | bytes 3342336 | tf_op jit(solution)/shard_map/all_gather | solution.py:90
  151.2 152.7 %all-gather.11.cloned.1.call-start = ((), (), s32[]{:S(2)}) async-start(), calls=%async_computation.7 | async-start | bytes 3342336 | tf_op jit(solution)/shard_map/all_gather | solution.py:91
  271.6 80.3 %all-to-all-start.5 = ((bf16[8,64,1,1536]{3,1,2,0:T(8,128)(2,1)}), bf16[8,64,1,1536]{3,1,2,0:T(8,128)(2,1)S(1)}, u32[]{:S(2)}, u32[]{:S(2)}) async-start(bf16[8,64,1,1536]{3,1,2,0:T(8,128)(2,1)} %bitcast.302), calls=%async_computation.5 | async-start | bytes 3145728 | tf_op jit(solution)/shard_map/all_to_all | solution.py:137
  351.9 29.4 %all-to-all-start.2 = ((bf16[8,64,1,1536]{3,1,2,0:T(8,128)(2,1)}), bf16[8,64,1,1536]{3,1,2,0:T(8,128)(2,1)}, u32[]{:S(2)}, u32[]{:S(2)}) async-start(bf16[8,64,1,1536]{3,1,2,0:T(8,128)(2,1)} %bitcast.303), calls=%async_computation.2 | async-start | bytes 3145728 | tf_op jit(solution)/shard_map/all_to_all | solution.py:137
Sparse Core Ops, SparseCore 0:
  147.5 38.4 all-gather.12
  187.7 35.9 all-gather.14
  225.3 35.9 all-gather.8
  262.8 41.0 all-gather.10
where the time goes:
time: 393 us; the launch traced here: 390 us
  waiting for transfers between devices  164 us (42%)
  matrix products  108 us (27%)
  starting transfers between devices  36.5 us (9%)
  blocking collectives  29.6 us (8%)
  other arithmetic  25.9 us (7%)
  between operations  13.6 us (3%)
  local copies, waits for them, and re-layouts  11.1 us (3%)
    all_gather x2, waiting for transfers between devices, one_sample(): value_tile = lax.all_gather(value_rows, 'seq', axis=2, tiled=True)  63.6 us
    all_to_all x3, waiting for transfers between devices, gather_batch(): lax.all_to_all(copies, 'batch', 0, 0, tiled=False)  51.4 us
    dot_general x32, matrix products, consume(): jnp.einsum('shqk,shdk->shdq', weights.astype(jnp.bfloat16), value_block,...  42.8 us
    dot_general x32, matrix products, consume(): jnp.einsum('shdq,shdk->shqk', query_heads, key_block, preferred_element_t...  40.8 us
    all_to_all x1, blocking collectives, gather_batch(): lax.all_to_all(copies, 'batch', 0, 0, tiled=False)  29.6 us
    all_gather x2, waiting for transfers between devices, one_sample(): key_tile = lax.all_gather(key_rows, 'seq', axis=2, tiled=True)  28.8 us
    all_to_all x2, waiting for transfers between devices, one_sample(): lax.all_to_all(partial_rows, 'batch', 0, 0, tiled=False).astype(jnp.float32)  20.4 us
    all_to_all x3, starting transfers between devices, gather_batch(): lax.all_to_all(copies, 'batch', 0, 0, tiled=False)  13.5 us
  transfers between devices with their start and end apart: 13, of which 7 were waited for; matrix products, arithmetic and copies ran while one was open for 32% of the time, Pallas kernels for 0%

commit v1 on v0

--- a/solution.py
+++ b/solution.py
@@ -87,7 +87,9 @@
     start_max = jnp.full((sample_count, heads_here, seq_rows), -jnp.inf, jnp.float32)
     start_sum = jnp.zeros((sample_count, heads_here, seq_rows), jnp.float32)
     start_acc = jnp.zeros((sample_count, heads_here, HD, seq_rows), jnp.float32)
-    key_tile = lax.all_gather(key_rows, "seq", axis=2, tiled=True)
+    key_tile = jnp.concatenate(
+        lax.all_to_all(jnp.stack([key_rows] * lax.axis_size("seq")), "seq", 0, 0), axis=2
+    )
     value_tile = lax.all_gather(value_rows, "seq", axis=2, tiled=True)
     key_count = key_tile.shape[2]
     block_rows = math.gcd(key_count, 512)

time: 393 us -> 425 us (1.081)
  local copies, waits for them, and re-layouts: 11.1 us -> 23.9 us
  waiting for transfers between devices: 164 us -> 175 us
  starting transfers between devices: 36.5 us -> 42.3 us
    all_to_all x0 -> x2, waiting for transfers between devices: none -> 98.2 us  [one_sample(): lax.all_to_all(jnp.stack([key_rows] * lax.axis_size('seq')), 'seq', 0, 0)]
    all_gather x2, waiting for transfers between devices: 63.6 us -> 0.02 us  [one_sample(): value_tile = lax.all_gather(value_rows, 'seq', axis=2, tiled=True)]
    all_gather x2 -> x0, waiting for transfers between devices: 28.8 us -> none  [one_sample(): key_tile = lax.all_gather(key_rows, 'seq', axis=2, tiled=True)]
    all_to_all x0 -> x2, starting transfers between devices: none -> 9.37 us  [one_sample(): lax.all_to_all(jnp.stack([key_rows] * lax.axis_size('seq')), 'seq', 0, 0)]
    reshape x0 -> x2, local copies, waits for them, and re-layouts: none -> 7.98 us  [one_sample(): jnp.concatenate(lax.all_to_all(jnp.stack([key_rows] * lax.axis_size('seq'...]
    all_to_all x3, waiting for transfers between devices: 51.4 us -> 59.4 us  [gather_batch(): lax.all_to_all(copies, 'batch', 0, 0, tiled=False)]
  transfers between devices with their start and end apart: 13 -> 13, of which waited for: 7 -> 6; matrix products, arithmetic and copies ran while one was open for 32% -> 34% of each run, Pallas kernels for 0% -> 0%
where the time goes in v1:
time: 425 us; the launch traced here: 421 us
  waiting for transfers between devices  175 us (41%)
  matrix products  109 us (26%)
  starting transfers between devices  42.3 us (10%)
  blocking collectives  29.6 us (7%)
  other arithmetic  26 us (6%)
  local copies, waits for them, and re-layouts  23.9 us (6%)
  between operations  13.9 us (3%)
    all_to_all x2, waiting for transfers between devices, one_sample(): lax.all_to_all(jnp.stack([key_rows] * lax.axis_size('seq')), 'seq', 0, 0)  98.2 us
    all_to_all x3, waiting for transfers between devices, gather_batch(): lax.all_to_all(copies, 'batch', 0, 0, tiled=False)  59.4 us
    dot_general x32, matrix products, consume(): jnp.einsum('shqk,shdk->shdq', weights.astype(jnp.bfloat16), value_block,...  42.7 us
    dot_general x32, matrix products, consume(): jnp.einsum('shdq,shdk->shqk', query_heads, key_block, preferred_element_t...  40.7 us
    all_to_all x1, blocking collectives, gather_batch(): lax.all_to_all(copies, 'batch', 0, 0, tiled=False)  29.6 us
    all_to_all x2, waiting for transfers between devices, one_sample(): lax.all_to_all(partial_rows, 'batch', 0, 0, tiled=False).astype(jnp.float32)  16.9 us
    dot_general x10, matrix products, one_sample(): jnp.einsum('std,ed->set', framed[:, offset:offset + seq_rows], conv_weigh...  12.8 us
    all_to_all x3, starting transfers between devices, gather_batch(): lax.all_to_all(copies, 'batch', 0, 0, tiled=False)  12.3 us
  transfers between devices with their start and end apart: 13, of which 6 were waited for; matrix products, arithmetic and copies ran while one was open for 34% of the time, Pallas kernels for 0%

profile of v1, /device:TPU:0, one launch (start us, length us, event | category | flops | bytes accessed | tf_op | source)
XLA Modules:
  0.0 421.2 jit_solution(14503390122080786499)
XLA Ops:
  7.8 29.6 %all_to_all.40 = bf16[8,1,64,1536]{3,2,1,0:T(8,128)(2,1)S(1)} all-to-all(bf16[8,1,64,1536]{3,2,1,0:T(8,128)(2,1)S(1)} %broadcast_in_dim.27), channel_id=1, replica_groups=mesh['seq'=16,'batch'=8] {'batch'}, dimensions={0} | all-to-all | bytes 3145728 | tf_op jit(solution)/shard_map/all_to_all | solution.py:30
  38.7 4.4 %all-to-all-start.4 = ((bf16[8,1,64,1536]{3,2,1,0:T(8,128)(2,1)}), bf16[8,1,64,1536]{3,2,1,0:T(8,128)(2,1)}, u32[]{:S(2)}, u32[]{:S(2)}) async-start(bf16[8,1,64,1536]{3,2,1,0:T(8,128)(2,1)} %broadcast_in_dim.33), calls=%async_computation.4 | async-start | bytes 3145728 | tf_op jit(solution)/shard_map/all_to_all | solution.py:30
  43.6 21.5 %all-to-all-done.4 = bf16[8,1,64,1536]{3,2,1,0:T(8,128)(2,1)} async-done(((bf16[8,1,64,1536]{3,2,1,0:T(8,128)(2,1)}), bf16[8,1,64,1536]{3,2,1,0:T(8,128)(2,1)}, u32[]{:S(2)}, u32[]{:S(2)}) %all-to-all-start.4) | async-done | bytes 1572896 | tf_op jit(solution)/shard_map/all_to_all | solution.py:30
  67.0 4.0 fusion.57
  72.3 3.0 collective-permute-start.2
  75.4 3.4 collective-permute-start
  80.1 4.8 %fusion.36 = (bf16[8,1,64,1536]{3,2,0,1:T(8,128)(2,1)}, bf16[8,1,64,1536]{3,2,0,1:T(8,128)(2,1)S(1)}) fusion(bf16[8,1,64,1536]{3,2,1,0:T(8,128)(2,1)S(1)} %all_to_all.40, f32[1536]{0:T(1024)S(1)} %copy-done.9, f32[8,64]{1,0:T(8,128)S(1)} %add_rsqrt_fusion.1, f32[8,64]{1,0:T(8,128)S(1)} %add_rsqrt_fusion, bf16[8,1,64,1536]{3,2,1,0:T(8,128)(2,1)} %all-to-all-done.4), kind=kLoop, calls=%fused_computation.54 | loop fusion | flops 18874368 | bytes 6301696 | tf_op jit(solution)/shard_map/convert_element_type | solution.py:57
  87.9 2.4 fusion.74
  94.2 4.3 %all-to-all-start.5 = ((bf16[8,1,192,512]{3,2,1,0:T(8,128)(2,1)}), bf16[8,1,192,512]{3,2,1,0:T(8,128)(2,1)}, u32[]{:S(2)}, u32[]{:S(2)}) async-start(bf16[8,1,192,512]{3,2,1,0:T(8,128)(2,1)} %broadcast_in_dim.61), calls=%async_computation.5 | async-start | bytes 3145728 | tf_op jit(solution)/shard_map/all_to_all | solution.py:30
  98.5 2.2 fusion.166
  101.1 2.3 fusion.101
  106.0 16.6 %all-to-all-done.5 = bf16[8,1,192,512]{3,2,1,0:T(8,128)(2,1)} async-done(((bf16[8,1,192,512]{3,2,1,0:T(8,128)(2,1)}), bf16[8,1,192,512]{3,2,1,0:T(8,128)(2,1)}, u32[]{:S(2)}, u32[]{:S(2)}) %all-to-all-start.5) | async-done | bytes 1572896 | tf_op jit(solution)/shard_map/all_to_all | solution.py:30
  124.0 3.6 all-to-all-start.1
  129.6 21.3 %all-to-all-done.1 = bf16[8,1,192,512]{3,2,1,0:T(8,128)(2,1)S(1)} async-done(((bf16[8,1,192,512]{3,2,1,0:T(8,128)(2,1)}), bf16[8,1,192,512]{3,2,1,0:T(8,128)(2,1)S(1)}, u32[]{:S(2)}, u32[]{:S(2)}) %all-to-all-start.1) | async-done | bytes 1572896 | tf_op jit(solution)/shard_map/all_to_all | solution.py:30
  151.3 2.0 bitcast_convert_fusion
  156.9 1.9 fusion.156
  158.8 1.9 stack.4
  160.7 4.9 %all-to-all-start.2 = ((bf16[16,1,192,512]{3,2,1,0:T(8,128)(2,1)}), bf16[16,1,192,512]{3,2,1,0:T(8,128)(2,1)}, u32[]{:S(2)}, u32[]{:S(2)}) async-start(bf16[16,1,192,512]{3,2,1,0:T(8,128)(2,1)} %stack.4), calls=%async_computation.2 | async-start | bytes 6291456 | tf_op jit(solution)/shard_map/all_to_all | solution.py:91
  166.1 55.9 %all-to-all-done.2 = bf16[16,1,192,512]{3,2,1,0:T(8,128)(2,1)} async-done(((bf16[16,1,192,512]{3,2,1,0:T(8,128)(2,1)}), bf16[16,1,192,512]{3,2,1,0:T(8,128)(2,1)}, u32[]{:S(2)}, u32[]{:S(2)}) %all-to-all-start.2) | async-done | bytes 3145760 | tf_op jit(solution)/shard_map/all_to_all | solution.py:91
  222.0 2.0 stack.5
  224.0 4.5 %all-to-all-start.6 = ((bf16[16,1,192,512]{3,2,1,0:T(8,128)(2,1)}), bf16[16,1,192,512]{3,2,1,0:T(8,128)(2,1)}, u32[]{:S(2)}, u32[]{:S(2)}) async-start(bf16[16,1,192,512]{3,2,1,0:T(8,128)(2,1)} %stack.5), calls=%async_computation.6 | async-start | bytes 6291456 | tf_op jit(solution)/shard_map/all_to_all | solution.py:91
  228.6 2.2 fusion.159
  230.9 2.1 fusion.149
  234.5 3.9 copy.46
  238.4 42.2 %all-to-all-done.6 = bf16[16,1,192,512]{3,2,1,0:T(8,128)(2,1)} async-done(((bf16[16,1,192,512]{3,2,1,0:T(8,128)(2,1)}), bf16[16,1,192,512]{3,2,1,0:T(8,128)(2,1)}, u32[]{:S(2)}, u32[]{:S(2)}) %all-to-all-start.6) | async-done | bytes 3145760 | tf_op jit(solution)/shard_map/all_to_all | solution.py:91
  280.7 4.0 copy.47
  284.7 46.1 %while.36 = (s32[]{:T(128)}, f32[1,1,512]{2,1,0:T(1,128)S(1)}, f32[1,1,512]{2,1,0:T(1,128)S(1)}, f32[1,1,192,512]{3,2,1,0:T(8,128)S(1)}, bf16[1,192,8192]{2,1,0:...) while((s32[]{:T(128)}, f32[1,1,512]{2,1,0:T(1,128)S(1)}, ...), condition=%wide.region_5.0_spmd.clone, body=%wide.region_2.0_spmd.clone.sunk | while | flops 202934784 | bytes 4554927 | solution.py:121
  330.9 1.9 convolution_convert_fusion.1
  332.7 4.3 %all-to-all-start.3 = ((bf16[8,64,1,1536]{3,1,2,0:T(8,128)(2,1)}), bf16[8,64,1,1536]{3,1,2,0:T(8,128)(2,1)}, u32[]{:S(2)}, u32[]{:S(2)}) async-start(bf16[8,64,1,1536]{3,1,2,0:T(8,128)(2,1)} %bitcast.33), calls=%async_computation.3 | async-start | bytes 3145728 | tf_op jit(solution)/shard_map/all_to_all | solution.py:139
  337.0 46.2 %while.37 = (s32[]{:T(128)}, f32[1,1,512]{2,1,0:T(1,128)S(1)}, f32[1,1,512]{2,1,0:T(1,128)S(1)}, f32[1,1,192,512]{3,2,1,0:T(8,128)S(1)}, bf16[1,192,8192]{2,1,0:...) while((s32[]{:T(128)}, f32[1,1,512]{2,1,0:T(1,128)S(1)}, ...), condition=%wide.region_12.0_spmd.clone, body=%wide.region_9.0_spmd.clone.sunk | while | flops 202934784 | bytes 4554927 | solution.py:121
  385.0 7.0 %all-to-all-start.7 = ((bf16[8,64,1,1536]{3,1,2,0:T(8,128)(2,1)}), bf16[8,64,1,1536]{3,1,2,0:T(8,128)(2,1)S(1)}, u32[]{:S(2)}, u32[]{:S(2)}) async-start(bf16[8,64,1,1536]{3,1,2,0:T(8,128)(2,1)} %bitcast.308), calls=%async_computation.7 | async-start | bytes 3145728 | tf_op jit(solution)/shard_map/all_to_all | solution.py:139
  396.5 16.9 %all-to-all-done.7 = bf16[8,64,1,1536]{3,1,2,0:T(8,128)(2,1)S(1)} async-done(((bf16[8,64,1,1536]{3,1,2,0:T(8,128)(2,1)}), bf16[8,64,1,1536]{3,1,2,0:T(8,128)(2,1)S(1)}, u32[]{:S(2)}, u32[]{:S(2)}) %all-to-all-start.7) | async-done | bytes 1572896 | tf_op jit(solution)/shard_map/all_to_all | solution.py:139
  (280 shorter events, 124.5 us)
Async XLA Ops:
  6.5 324.3 %copy-start = (bf16[192,1536]{1,0:T(8,128)(2,1)S(1)}, bf16[192,1536]{1,0:T(8,128)(2,1)}, u32[]{:S(2)}) copy-start(bf16[192,1536]{1,0:T(8,128)(2,1)} %param.19) | copy-start | bytes 1769476
  38.7 28.2 %copy-start.9 = (f32[1536]{0:T(1024)S(1)}, f32[1536]{0:T(1024)}, u32[]{:S(2)}) copy-start(f32[1536]{0:T(1024)} %param.13) | copy-start | bytes 18436
  38.7 26.4 %all-to-all-start.4 = ((bf16[8,1,64,1536]{3,2,1,0:T(8,128)(2,1)}), bf16[8,1,64,1536]{3,2,1,0:T(8,128)(2,1)}, u32[]{:S(2)}, u32[]{:S(2)}) async-start(bf16[8,1,64,1536]{3,2,1,0:T(8,128)(2,1)} %broadcast_in_dim.33), calls=%async_computation.4 | async-start | bytes 3145728 | tf_op jit(solution)/shard_map/all_to_all | solution.py:30
  71.0 13.9 %copy-start.5 = (bf16[1,512,1536]{2,1,0:T(8,128)(2,1)}, bf16[1,512,1536]{2,1,0:T(8,128)(2,1)S(1)}, u32[]{:S(2)}) copy-start(bf16[1,512,1536]{2,1,0:T(8,128)(2,1)S(1)} %get-tuple-element.353) | copy-start | bytes 4718596
  71.0 13.9 %copy-start.7 = (bf16[1,512,1536]{2,1,0:T(8,128)(2,1)}, bf16[1,512,1536]{2,1,0:T(8,128)(2,1)S(1)}, u32[]{:S(2)}) copy-start(bf16[1,512,1536]{2,1,0:T(8,128)(2,1)S(1)} %get-tuple-element.354) | copy-start | bytes 4718596
  71.0 16.9 %collective-permute-start.3 = (bf16[1,2,1536]{2,1,0:T(2,128)(2,1)S(1)}, bf16[1,2,1536]{2,1,0:T(2,128)(2,1)S(1)}, u32[]{:S(2)}, u32[]{:S(2)}) collective-permute-start(bf16[1,2,1536]{2,1,0:T(2,128)(2,1)S(1)} %get-tuple-element.346), channel_id=1, source_target_pairs={{8,0},{16,8},{24,16},{32,24},{40,32},{48,40},{56,48},{64,56},{72,6... | collective-permute-start | bytes 18440 | tf_op jit(solution)/shard_map/ppermute | solution.py:20
  72.3 19.2 %collective-permute-start.2 = (bf16[1,2,1536]{2,1,0:T(2,128)(2,1)S(1)}, bf16[1,2,1536]{2,1,0:T(2,128)(2,1)S(1)}, u32[]{:S(2)}, u32[]{:S(2)}) collective-permute-start(bf16[1,2,1536]{2,1,0:T(2,128)(2,1)S(1)} %get-tuple-element.345), channel_id=1, source_target_pairs={{0,8},{8,16},{16,24},{24,32},{32,40},{40,48},{48,56},{56,64},{64,7... | collective-permute-start | bytes 18440 | tf_op jit(solution)/shard_map/ppermute | solution.py:18
  75.4 25.7 %collective-permute-start = (bf16[1,2,1536]{2,1,0:T(2,128)(2,1)S(1)}, bf16[1,2,1536]{2,1,0:T(2,128)(2,1)S(1)}, u32[]{:S(2)}, u32[]{:S(2)}) collective-permute-start(bf16[1,2,1536]{2,1,0:T(2,128)(2,1)S(1)} %get-tuple-element.343), channel_id=1, source_target_pairs={{0,8},{8,16},{16,24},{24,32},{32,40},{40,48},{48,56},{56,64},{64,7... | collective-permute-start | bytes 18440 | tf_op jit(solution)/shard_map/ppermute | solution.py:18
  78.8 24.6 %collective-permute-start.1 = (bf16[1,2,1536]{2,1,0:T(2,128)(2,1)S(1)}, bf16[1,2,1536]{2,1,0:T(2,128)(2,1)S(1)}, u32[]{:S(2)}, u32[]{:S(2)}) collective-permute-start(bf16[1,2,1536]{2,1,0:T(2,128)(2,1)S(1)} %get-tuple-element.344), channel_id=1, source_target_pairs={{8,0},{16,8},{24,16},{32,24},{40,32},{48,40},{56,48},{64,56},{72,6... | collective-permute-start | bytes 18440 | tf_op jit(solution)/shard_map/ppermute | solution.py:20
  87.9 2.4 copy-start.8
  87.9 3.0 copy-start.11
  94.2 28.4 %all-to-all-start.5 = ((bf16[8,1,192,512]{3,2,1,0:T(8,128)(2,1)}), bf16[8,1,192,512]{3,2,1,0:T(8,128)(2,1)}, u32[]{:S(2)}, u32[]{:S(2)}) async-start(bf16[8,1,192,512]{3,2,1,0:T(8,128)(2,1)} %broadcast_in_dim.61), calls=%async_computation.5 | async-start | bytes 3145728 | tf_op jit(solution)/shard_map/all_to_all | solution.py:30
  100.9 2.5 copy-start.6
  101.0 2.9 copy-start.12
  124.0 26.9 %all-to-all-start.1 = ((bf16[8,1,192,512]{3,2,1,0:T(8,128)(2,1)}), bf16[8,1,192,512]{3,2,1,0:T(8,128)(2,1)S(1)}, u32[]{:S(2)}, u32[]{:S(2)}) async-start(bf16[8,1,192,512]{3,2,1,0:T(8,128)(2,1)} %broadcast_in_dim.29), calls=%async_computation.1 | async-start | bytes 3145728 | tf_op jit(solution)/shard_map/all_to_all | solution.py:30
  127.6 157.1 %all-gather.5.cloned.1.call-start = ((), (), s32[]{:S(2)}) async-start(), calls=%async_computation.8 | async-start | bytes 3342336 | tf_op jit(solution)/shard_map/all_gather | solution.py:93
  150.9 2.4 copy-start.2
  153.3 0.7 copy-start.10
  154.0 1.7 copy-start.4
  154.0 2.9 copy-start.3
  154.6 1.1 copy-start.1
  160.7 61.3 %all-to-all-start.2 = ((bf16[16,1,192,512]{3,2,1,0:T(8,128)(2,1)}), bf16[16,1,192,512]{3,2,1,0:T(8,128)(2,1)}, u32[]{:S(2)}, u32[]{:S(2)}) async-start(bf16[16,1,192,512]{3,2,1,0:T(8,128)(2,1)} %stack.4), calls=%async_computation.2 | async-start | bytes 6291456 | tf_op jit(solution)/shard_map/all_to_all | solution.py:91
  224.0 56.7 %all-to-all-start.6 = ((bf16[16,1,192,512]{3,2,1,0:T(8,128)(2,1)}), bf16[16,1,192,512]{3,2,1,0:T(8,128)(2,1)}, u32[]{:S(2)}, u32[]{:S(2)}) async-start(bf16[16,1,192,512]{3,2,1,0:T(8,128)(2,1)} %stack.5), calls=%async_computation.6 | async-start | bytes 6291456 | tf_op jit(solution)/shard_map/all_to_all | solution.py:91
  228.5 108.5 %all-gather.7.cloned.1.call-start = ((), (), s32[]{:S(2)}) async-start(), calls=%async_computation.9 | async-start | bytes 3342336 | tf_op jit(solution)/shard_map/all_gather | solution.py:93
  332.7 52.3 %all-to-all-start.3 = ((bf16[8,64,1,1536]{3,1,2,0:T(8,128)(2,1)}), bf16[8,64,1,1536]{3,1,2,0:T(8,128)(2,1)}, u32[]{:S(2)}, u32[]{:S(2)}) async-start(bf16[8,64,1,1536]{3,1,2,0:T(8,128)(2,1)} %bitcast.33), calls=%async_computation.3 | async-start | bytes 3145728 | tf_op jit(solution)/shard_map/all_to_all | solution.py:139
  385.0 28.3 %all-to-all-start.7 = ((bf16[8,64,1,1536]{3,1,2,0:T(8,128)(2,1)}), bf16[8,64,1,1536]{3,1,2,0:T(8,128)(2,1)S(1)}, u32[]{:S(2)}, u32[]{:S(2)}) async-start(bf16[8,64,1,1536]{3,1,2,0:T(8,128)(2,1)} %bitcast.308), calls=%async_computation.7 | async-start | bytes 3145728 | tf_op jit(solution)/shard_map/all_to_all | solution.py:139
Sparse Core Ops, SparseCore 0:
  157.0 64.2 all-gather.4
  231.0 56.9 all-gather.6
